TPU v7x, 512 devices: a whole 4x4x16 slice. The times are simulated.
512 devices in a mesh: grp: 4 (over y), seq: 32 (over z, core), mp: 4 (over x).
Axes of the slice: x: 4, y: 4, z: 16, core: 2. Of those that a mesh axis runs over, the one named last changes fastest.
Arguments:
- queries: bfloat16 [4, 4096, 2048], P('grp', 'seq', 'mp'), may hold values from -16 to 16
- d_out: bfloat16 [4, 4096, 2048], P('grp', 'seq', 'mp'), may hold values from -6 to 6
- neighbour_kv: bfloat16 [4, 256, 128, 2, 2048], P('grp', 'seq', None, None, 'mp'), may hold values from -16 to 16
- target: int32 [4, 256], P('grp', 'seq'), may hold values from -1 to 127, as said below
- bias: float32 [16, 191], P('mp'), may hold values from -6 to 6
Outputs:
- attended: bfloat16 [4, 4096, 2048], P('grp', 'seq', 'mp')
- d_query: bfloat16 [4, 4096, 2048], P('grp', 'seq', 'mp')
- d_kv: bfloat16 [4, 256, 128, 2, 2048], P('grp', 'seq', None, None, 'mp')
- d_bias: float32 [16, 191], P('mp')
Inputs may be any that keep to these rules, and one draw needn't show every extreme that they name: `target`: in each group every entry 0..127 stands in exactly one slot and -1 marks an empty slot. The slots of one index of seq hold at most 1 entries e with the same e // 4, and some index reaches that; some index of seq holds 8 entries.
All inputs are finite; a program needn't handle non-finite values.
Results may differ from a plain program's by a relative error of at most 0.011.
Values may be sent and summed in bfloat16 or wider, within the bound.
No kernel may reach another device: no remote copies, remote signals or barrier semaphores. Data moves between devices by JAX's collectives and lax.ppermute only.
A program may use at most 128 MiB of HBM per device.

v0:
```python
import jax
import jax.numpy as jnp
from jax import lax
from jax.sharding import PartitionSpec as P

STRETCH = 64
NB_LEN = 128


def passed_along(block, axis, distance):
    devices = range(lax.axis_size(axis))
    route = [(i - distance, i) for i in devices if i - distance in devices]
    return lax.ppermute(block, axis, route)


def bias_grid(lookup, row_count, col_count):
    head_num = lookup.shape[0]
    span = row_count + col_count
    padded = jnp.pad(lookup, ((0, 0), (0, 1)))
    flattened = jnp.tile(padded, (1, row_count))
    flattened = jnp.pad(flattened, ((0, 0), (0, row_count)))
    shaped = flattened.reshape(head_num, row_count, span + 1)[:, :, :col_count]
    return shaped[:, :, ::-1]


def bias_fold(grads):
    head_num, row_count, col_count = grads.shape
    turned = grads[:, :, ::-1]
    padded = jnp.pad(turned, ((0, 0), (0, 0), (0, row_count)))
    flattened = padded.reshape(head_num, row_count * (row_count + col_count))
    flattened = flattened[:, : row_count * (row_count + col_count - 1)]
    return jnp.sum(flattened.reshape(head_num, row_count, row_count + col_count - 1), axis=1)


def select_rows(picker, lookup):
    chosen = jnp.dot(
        picker.astype(lookup.dtype),
        lookup,
        preferred_element_type=jnp.float32,
        precision=lax.Precision.HIGHEST,
    )
    return chosen.astype(lookup.dtype)


def slot_places(target_row, owners, capacity, per_owner):
    is_used = target_row >= 0
    owner_of = jnp.where(is_used, target_row // per_owner, -1)
    positions = jnp.arange(target_row.shape[0])
    earlier = (
        (positions[None, :] < positions[:, None])
        & (owner_of[None, :] == owner_of[:, None])
        & is_used[None, :]
    )
    rank_of = jnp.sum(earlier.astype(jnp.int32), axis=1)
    match_owner = owner_of[None, :] == jnp.arange(owners)[:, None]
    match_rank = rank_of[None, :] == jnp.arange(capacity)[:, None]
    return match_owner[:, None, :] & match_rank[None, :, :] & is_used[None, None, :]


def local(queries, d_out, neighbour_kv, target, bias):
    tok_rows = queries.shape[1]
    width_dev = queries.shape[2]
    head_count = bias.shape[0]
    head_depth = width_dev // head_count
    stretch_count = tok_rows // STRETCH
    per_owner = 2 * stretch_count
    shard_count = lax.axis_size("seq")
    my_index = lax.axis_index("seq")
    group_size = min(shard_count, per_owner)
    capacity = (per_owner + group_size - 1) // group_size
    seq_stretches = min(2048, tok_rows * shard_count) // STRETCH
    scale_factor = head_depth ** (-0.5)
    bias_rows = bias_grid(bias, STRETCH, NB_LEN).transpose(1, 0, 2)
    q_rows = queries[0]
    g_rows = d_out[0]
    next_pair = passed_along(jnp.stack([q_rows[:STRETCH], g_rows[:STRETCH]]), "seq", -1)
    row_ids = jnp.arange(STRETCH)
    stretch_ids = my_index * stretch_count + jnp.arange(stretch_count)
    is_live = (row_ids[None, :] == 0) | ((stretch_ids[:, None] + 1) % seq_stretches != 0)
    live_rows = is_live.astype(jnp.float32)
    q_win = jnp.concatenate([q_rows, next_pair[0]])[STRETCH - 1 : STRETCH - 1 + tok_rows]
    q_win = q_win.reshape(stretch_count, STRETCH * width_dev)
    g_win = jnp.concatenate([g_rows, next_pair[1]])[STRETCH - 1 : STRETCH - 1 + tok_rows]
    g_win = g_win.reshape(stretch_count, STRETCH, width_dev) * is_live[:, :, None].astype(
        jnp.bfloat16
    )
    g_win = g_win.reshape(stretch_count, STRETCH * width_dev)
    my_targets = target[0]
    slot_count = my_targets.shape[0]
    send_map = slot_places(my_targets, shard_count, capacity, per_owner)
    id_buffer = jnp.sum(jnp.where(send_map, my_targets[None, None, :] + 1, 0), axis=2) - 1
    recv_ids = lax.all_to_all(id_buffer, "seq", split_axis=0, concat_axis=0, tiled=True)
    flat_ids = recv_ids.reshape(shard_count * capacity)
    has_entry = flat_ids >= 0
    local_entry = flat_ids - my_index * per_owner
    entry_pick = (local_entry[:, None] == jnp.arange(per_owner)[None, :]) & has_entry[:, None]
    stretch_pick = (local_entry[:, None] // 2 == jnp.arange(stretch_count)[None, :]) & has_entry[
        :, None
    ]
    back_pick = send_map.reshape(shard_count * capacity, slot_count)
    slot_pick = back_pick.T
    q_send = select_rows(stretch_pick, q_win).reshape(shard_count, capacity, STRETCH * width_dev)
    g_send = select_rows(stretch_pick, g_win).reshape(shard_count, capacity, STRETCH * width_dev)
    q_recv, g_recv = (
        lax.all_to_all(q_send, "seq", split_axis=0, concat_axis=0, tiled=True),
        lax.all_to_all(g_send, "seq", split_axis=0, concat_axis=0, tiled=True),
    )
    q_slots = select_rows(slot_pick, q_recv.reshape(shard_count * capacity, -1))
    q_slots = q_slots.reshape(slot_count, STRETCH, head_count, head_depth)
    stored = neighbour_kv[0]
    key_rows = stored[:, :, 0].reshape(slot_count, NB_LEN, head_count, head_depth)
    value_rows = stored[:, :, 1].reshape(slot_count, NB_LEN, head_count, head_depth)
    scores = jnp.einsum("sihd,sjhd->sihj", q_slots, key_rows, preferred_element_type=jnp.float32)
    scores = scores * scale_factor + bias_rows[None]
    peak_val = jnp.max(scores, axis=-1)
    weights = jnp.exp(scores - peak_val[..., None])
    row_total = jnp.sum(weights, axis=-1)
    partial_value = jnp.einsum(
        "sihj,sjhd->sihd",
        weights.astype(jnp.bfloat16),
        value_rows,
        preferred_element_type=jnp.float32,
    )
    part_send = select_rows(back_pick, partial_value.reshape(slot_count, -1)).reshape(
        shard_count, capacity, -1
    )
    peak_send = select_rows(back_pick, peak_val.reshape(slot_count, -1)).reshape(
        shard_count, capacity, -1
    )
    total_send = select_rows(back_pick, row_total.reshape(slot_count, -1)).reshape(
        shard_count, capacity, -1
    )
    part_recv, peak_recv, total_recv = (
        lax.all_to_all(part_send, "seq", split_axis=0, concat_axis=0, tiled=True),
        lax.all_to_all(peak_send, "seq", split_axis=0, concat_axis=0, tiled=True),
        lax.all_to_all(total_send, "seq", split_axis=0, concat_axis=0, tiled=True),
    )
    entry_back = entry_pick.T
    parts_own = select_rows(entry_back, part_recv.reshape(shard_count * capacity, -1))
    parts_own = parts_own.reshape(stretch_count, 2, STRETCH, head_count, head_depth)
    peaks_own = select_rows(entry_back, peak_recv.reshape(shard_count * capacity, -1))
    peaks_own = peaks_own.reshape(stretch_count, 2, STRETCH, head_count)
    totals_own = select_rows(entry_back, total_recv.reshape(shard_count * capacity, -1))
    totals_own = totals_own.reshape(stretch_count, 2, STRETCH, head_count)
    top_peak = jnp.max(peaks_own, axis=1)
    factor = jnp.exp(peaks_own - top_peak[:, None])
    denominator = jnp.sum(factor * totals_own, axis=1)
    combined = jnp.sum(factor[..., None] * parts_own, axis=1) / denominator[..., None]
    combined = combined * live_rows[:, :, None, None]
    att_win = combined.astype(jnp.bfloat16).reshape(tok_rows, width_dev)
    att_before = passed_along(att_win[tok_rows - STRETCH :], "seq", 1)
    log_total = top_peak + jnp.log(denominator)
    g_wide = g_win.reshape(stretch_count, STRETCH, head_count, head_depth).astype(jnp.float32)
    inner_dot = jnp.sum(g_wide * combined, axis=-1)
    row_stats = jnp.repeat(jnp.stack([log_total, inner_dot], axis=1), 2, axis=0)
    stats_send = select_rows(entry_pick, row_stats.reshape(per_owner, -1)).reshape(
        shard_count, capacity, -1
    )
    stats_recv = lax.all_to_all(stats_send, "seq", split_axis=0, concat_axis=0, tiled=True)
    g_slots = select_rows(slot_pick, g_recv.reshape(shard_count * capacity, -1))
    g_slots = g_slots.reshape(slot_count, STRETCH, head_count, head_depth)
    stats_slots = select_rows(slot_pick, stats_recv.reshape(shard_count * capacity, -1))
    stats_slots = stats_slots.reshape(slot_count, 2, STRETCH, head_count)
    prob_full = jnp.exp(scores - stats_slots[:, 0][..., None])
    prob_low = prob_full.astype(jnp.bfloat16)
    grad_values = jnp.einsum(
        "sihj,sihd->sjhd", prob_low, g_slots, preferred_element_type=jnp.float32
    )
    grad_prob = jnp.einsum(
        "sihd,sjhd->sihj", g_slots, value_rows, preferred_element_type=jnp.float32
    )
    grad_scores = prob_full * (grad_prob - stats_slots[:, 1][..., None])
    scores_low = grad_scores.astype(jnp.bfloat16)
    grad_rows = (
        jnp.einsum("sihj,sjhd->sihd", scores_low, key_rows, preferred_element_type=jnp.float32)
        * scale_factor
    )
    grad_keys = (
        jnp.einsum("sihj,sihd->sjhd", scores_low, q_slots, preferred_element_type=jnp.float32)
        * scale_factor
    )
    d_kv = jnp.stack(
        [
            grad_keys.reshape(slot_count, NB_LEN, width_dev),
            grad_values.reshape(slot_count, NB_LEN, width_dev),
        ],
        axis=2,
    ).astype(jnp.bfloat16)
    bias_part = bias_fold(jnp.sum(grad_scores, axis=0).transpose(1, 0, 2))
    rows_send = select_rows(back_pick, grad_rows.reshape(slot_count, -1)).reshape(
        shard_count, capacity, -1
    )
    rows_recv = lax.all_to_all(rows_send, "seq", split_axis=0, concat_axis=0, tiled=True)
    grad_entries = select_rows(entry_back, rows_recv.reshape(shard_count * capacity, -1))
    grad_entries = grad_entries.reshape(stretch_count, 2, STRETCH * width_dev)
    grad_win = (
        (grad_entries[:, 0] + grad_entries[:, 1]).astype(jnp.bfloat16).reshape(tok_rows, width_dev)
    )
    grad_before = passed_along(grad_win[tok_rows - STRETCH :], "seq", 1)
    attended = jnp.concatenate([att_before[1:], att_win[: tok_rows - STRETCH + 1]])
    d_query = jnp.concatenate([grad_before[1:], grad_win[: tok_rows - STRETCH + 1]])
    raw_sum = lax.psum(bias_part, ("grp", "seq"))
    squares = lax.psum(jnp.sum(raw_sum * raw_sum), "mp")
    d_bias = raw_sum * jnp.minimum(1.0, 1.0 / jnp.sqrt(squares + 1e-12))
    return (attended[None], d_query[None], d_kv[None], d_bias)


def solution(mesh):
    in_specs = (
        P("grp", "seq", "mp"),
        P("grp", "seq", "mp"),
        P("grp", "seq", None, None, "mp"),
        P("grp", "seq"),
        P("mp", None),
    )
    out_specs = (
        P("grp", "seq", "mp"),
        P("grp", "seq", "mp"),
        P("grp", "seq", None, None, "mp"),
        P("mp", None),
    )
    return jax.shard_map(local, mesh=mesh, in_specs=in_specs, out_specs=out_specs, check_vma=False)
```

profile of v0, /device:TPU:1, one launch (start us, length us, event | category | flops | bytes accessed | tf_op | source)
XLA Modules:
  0.0 1025.3 jit_solution(9001594490378168722)
XLA Ops:
  4.3 16.7 %all-to-all-start = ((s32[32,1,1]{2,1,0:T(1,128)}), s32[32,1,1]{2,1,0:T(1,128)S(1)}, u32[]{:S(2)}, u32[]{:S(2)}) async-start(s32[32,1,1]{2,1,0:T(1,128)} %copy.156), calls=%async_computation | async-start | bytes 32768 | tf_op jit(solution)/shard_map/all_to_all | solution.py:92
  22.7 2.1 collective-permute-start
  24.9 7.8 all-to-all-done
  36.4 2.9 reduce.9
  39.3 4.5 reshape.685
  43.8 6.9 all-to-all-start.1
  51.2 2.1 fusion.1
  53.3 4.5 reduce.10
  57.8 4.5 reshape.687
  62.3 87.0 %all-to-all-done.1 = bf16[32,2,16384]{2,1,0:T(2,128)(2,1)S(1)} async-done(((bf16[32,2,16384]{2,1,0:T(2,128)(2,1)}), bf16[32,2,16384]{2,1,0:T(2,128)(2,1)S(1)}, u32[]{:S(2)}, u32[]{:S(2)}) %all-to-all-start.1) | async-done | bytes 2097184 | tf_op jit(solution)/shard_map/all_to_all | solution.py:105
  149.3 5.2 all-to-all-start.6
  154.5 6.2 copy.158
  161.5 2.7 fusion.78
  164.1 10.5 %reshape.686 = bf16[32,1,32768]{2,1,0:T(2,128)(2,1)} reshape(bf16[32,2,16384]{2,1,0:T(2,128)(2,1)} %copy-done) | data formatting | bytes 4194304
  174.6 4.5 convolution_convert_fusion.3
  179.9 1.9 fusion.79
  182.7 1.8 convolution_bitcast_fusion.3
  184.6 69.2 %all-to-all-done.6 = bf16[32,2,16384]{2,1,0:T(2,128)(2,1)} async-done(((bf16[32,2,16384]{2,1,0:T(2,128)(2,1)}), bf16[32,2,16384]{2,1,0:T(2,128)(2,1)}, u32[]{:S(2)}, u32[]{:S(2)}) %all-to-all-start.6) | async-done | bytes 2097184 | tf_op jit(solution)/shard_map/all_to_all | solution.py:106
  253.8 6.3 all-to-all-start.2
  260.7 2.9 copy.167
  263.6 2.7 reshape.655
  267.3 5.0 all-to-all-done.2
  272.3 7.3 all-to-all-start.4
  279.6 3.1 convolution_bitcast_fusion.1
  282.7 6.3 copy.168
  289.0 2.7 all-to-all-done.4
  291.7 9.9 all-to-all-start.3
  301.7 10.5 %reshape.688 = bf16[32,1,32768]{2,1,0:T(2,128)(2,1)} reshape(bf16[32,2,16384]{2,1,0:T(2,128)(2,1)} %all-to-all-done.6) | data formatting | bytes 4194304
  313.4 171.4 %all-to-all-done.3 = f32[32,1,32768]{2,1,0:T(1,128)} async-done(((f32[32,1,32768]{2,1,0:T(1,128)}), f32[32,1,32768]{2,1,0:T(1,128)}, u32[]{:S(2)}, u32[]{:S(2)}) %all-to-all-start.3) | async-done | bytes 4194336 | tf_op jit(solution)/shard_map/all_to_all | solution.py:134
  484.7 6.6 copy.249
  491.3 6.0 dot_general.86
  497.4 6.8 fusion.20
  506.6 10.9 %all-to-all-start.5 = ((f32[32,1,512]{2,1,0:T(1,128)}), f32[32,1,512]{2,1,0:T(1,128)S(1)}, u32[]{:S(2)}, u32[]{:S(2)}) async-start(f32[32,1,512]{2,1,0:T(1,128)} %copy.177), calls=%async_computation.5 | async-start | bytes 131072 | tf_op jit(solution)/shard_map/all_to_all | solution.py:159
  517.5 4.5 convolution_convert_fusion.2
  522.0 8.5 all-to-all-done.5
  532.7 2.0 fusion.12
  537.0 3.1 convolution_bitcast_fusion
  540.1 6.3 copy.187
  546.4 6.1 all-to-all-start.7
  552.9 3.7 collective-permute-start.1
  556.7 169.2 %collective-permute-done.1 = bf16[64,512]{1,0:T(8,128)(2,1)S(1)} collective-permute-done((bf16[64,512]{1,0:T(8,128)(2,1)S(1)}, bf16[64,512]{1,0:T(8,128)(2,1)S(1)}, u32[]{:S(2)}, u32[]{:S(2)}) %collective-permute-start.1) | collective-permute-done | bytes 65568 | tf_op jit(solution)/shard_map/ppermute | solution.py:13
  726.5 256.5 %psum.14 = f32[4,191]{1,0:T(4,128)S(1)} all-reduce(f32[4,191]{1,0:T(4,128)S(1)} %reduce_sum.88), channel_id=1, replica_groups=mesh['grp'=4,'seq'=32,'mp'=4] {'grp','seq'}, use_global_device_ids=true, to_apply=%region_10.11 | all-reduce | flops 764 | bytes 6112 | tf_op jit(solution)/shard_map/psum | solution.py:202
  984.3 9.1 psum.15
  995.2 4.6 copy.191
  1001.6 3.8 copy.190
  1006.1 6.7 pad_maximum_fusion
  1012.8 6.0 fusion.2
  1020.3 1.9 collective-permute-start.2
  (115 shorter events, 31.8 us)
Async XLA Ops:
  4.3 28.5 %all-to-all-start = ((s32[32,1,1]{2,1,0:T(1,128)}), s32[32,1,1]{2,1,0:T(1,128)S(1)}, u32[]{:S(2)}, u32[]{:S(2)}) async-start(s32[32,1,1]{2,1,0:T(1,128)} %copy.156), calls=%async_computation | async-start | bytes 32768 | tf_op jit(solution)/shard_map/all_to_all | solution.py:92
  22.7 11.4 %collective-permute-start = (bf16[2,64,512]{2,1,0:T(8,128)(2,1)S(1)}, bf16[2,64,512]{2,1,0:T(8,128)(2,1)S(1)}, u32[]{:S(2)}, u32[]{:S(2)}) collective-permute-start(bf16[2,64,512]{2,1,0:T(8,128)(2,1)S(1)} %pad_maximum_fusion.3), channel_id=1, source_target_pairs={{4,0},{8,4},{12,8},{16,12},{20,16},{24,20},{28,24},{32,28},{36,32}... | collective-permute-start | bytes 393224 | tf_op jit(solution)/shard_map/ppermute | solution.py:13
  39.3 11.7 %copy-start.5 = (bf16[1,128,512]{2,1,0:T(8,128)(2,1)S(1)}, bf16[1,128,512]{2,1,0:T(8,128)(2,1)}, u32[]{:S(2)}) copy-start(bf16[1,128,512]{2,1,0:T(8,128)(2,1)} %param.6) | copy-start | bytes 393220
  43.8 105.5 %all-to-all-start.1 = ((bf16[32,2,16384]{2,1,0:T(2,128)(2,1)}), bf16[32,2,16384]{2,1,0:T(2,128)(2,1)S(1)}, u32[]{:S(2)}, u32[]{:S(2)}) async-start(bf16[32,2,16384]{2,1,0:T(2,128)(2,1)} %reshape.685), calls=%async_computation.1 | async-start | bytes 4194304 | tf_op jit(solution)/shard_map/all_to_all | solution.py:105
  62.3 98.4 %copy-start.7 = (f32[4,191]{1,0:T(4,128)S(1)}, f32[4,191]{1,0:T(4,128)}, u32[]{:S(2)}) copy-start(f32[4,191]{1,0:T(4,128)} %param.9) | copy-start | bytes 9172
  149.3 11.4 %copy-start = (bf16[32,2,16384]{2,1,0:T(2,128)(2,1)}, bf16[32,2,16384]{2,1,0:T(2,128)(2,1)S(1)}, u32[]{:S(2)}) copy-start(bf16[32,2,16384]{2,1,0:T(2,128)(2,1)S(1)} %all-to-all-done.1) | copy-start | bytes 6291460
  149.3 104.5 %all-to-all-start.6 = ((bf16[32,2,16384]{2,1,0:T(2,128)(2,1)}), bf16[32,2,16384]{2,1,0:T(2,128)(2,1)}, u32[]{:S(2)}, u32[]{:S(2)}) async-start(bf16[32,2,16384]{2,1,0:T(2,128)(2,1)} %reshape.687), calls=%async_computation.6 | async-start | bytes 4194304 | tf_op jit(solution)/shard_map/all_to_all | solution.py:106
  179.1 0.8 copy-start.4
  253.8 18.5 %all-to-all-start.2 = ((f32[32,1,256]{2,1,0:T(1,128)}), f32[32,1,256]{2,1,0:T(1,128)S(1)}, u32[]{:S(2)}, u32[]{:S(2)}) async-start(f32[32,1,256]{2,1,0:T(1,128)} %copy.162), calls=%async_computation.2 | async-start | bytes 65536 | tf_op jit(solution)/shard_map/all_to_all | solution.py:135
  272.3 19.4 %all-to-all-start.4 = ((f32[32,1,256]{2,1,0:T(1,128)}), f32[32,1,256]{2,1,0:T(1,128)S(1)}, u32[]{:S(2)}, u32[]{:S(2)}) async-start(f32[32,1,256]{2,1,0:T(1,128)} %copy.171), calls=%async_computation.4 | async-start | bytes 65536 | tf_op jit(solution)/shard_map/all_to_all | solution.py:136
  291.7 193.0 %all-to-all-start.3 = ((f32[32,1,32768]{2,1,0:T(1,128)}), f32[32,1,32768]{2,1,0:T(1,128)}, u32[]{:S(2)}, u32[]{:S(2)}) async-start(f32[32,1,32768]{2,1,0:T(1,128)} %copy.168), calls=%async_computation.3 | async-start | bytes 8388608 | tf_op jit(solution)/shard_map/all_to_all | solution.py:134
  506.6 23.9 %all-to-all-start.5 = ((f32[32,1,512]{2,1,0:T(1,128)}), f32[32,1,512]{2,1,0:T(1,128)S(1)}, u32[]{:S(2)}, u32[]{:S(2)}) async-start(f32[32,1,512]{2,1,0:T(1,128)} %copy.177), calls=%async_computation.5 | async-start | bytes 131072 | tf_op jit(solution)/shard_map/all_to_all | solution.py:159
  522.0 13.5 %copy-start.1 = (bf16[8,32768]{1,0:T(8,128)(2,1)}, bf16[8,32768]{1,0:T(8,128)(2,1)S(1)}, u32[]{:S(2)}) copy-start(bf16[8,32768]{1,0:T(8,128)(2,1)S(1)} %convolution_convert_fusion.2) | copy-start | bytes 1572868
  531.9 0.8 copy-start.3
  546.4 6.4 copy-start.6
  546.4 447.1 %copy-start.2 = (bf16[8,32768]{1,0:T(8,128)(2,1)S(1)}, bf16[8,32768]{1,0:T(8,128)(2,1)}, u32[]{:S(2)}) copy-start(bf16[8,32768]{1,0:T(8,128)(2,1)} %copy-done.1) | copy-start | bytes 1572868
  546.4 466.4 %all-to-all-start.7 = ((f32[32,1,32768]{2,1,0:T(1,128)}), f32[32,1,32768]{2,1,0:T(1,128)}, u32[]{:S(2)}, u32[]{:S(2)}) async-start(f32[32,1,32768]{2,1,0:T(1,128)} %copy.187), calls=%async_computation.7 | async-start | bytes 8388608 | tf_op jit(solution)/shard_map/all_to_all | solution.py:193
  552.9 173.0 %collective-permute-start.1 = (bf16[64,512]{1,0:T(8,128)(2,1)S(1)}, bf16[64,512]{1,0:T(8,128)(2,1)S(1)}, u32[]{:S(2)}, u32[]{:S(2)}) collective-permute-start(bf16[64,512]{1,0:T(8,128)(2,1)S(1)} %bitcast.224), channel_id=1, source_target_pairs={{0,4},{4,8},{8,12},{12,16},{16,20},{20,24},{24,28},{28,32},{32,36}... | collective-permute-start | bytes 196616 | tf_op jit(solution)/shard_map/ppermute | solution.py:13
  1020.3 4.2 collective-permute-start.2
where the time goes:
time: 1040 us; the launch traced here: 1030 us
  waiting for transfers between devices  522 us (50%)
  blocking collectives  266 us (26%)
  local copies, waits for them, and re-layouts  90.5 us (9%)
  starting transfers between devices  77.1 us (7%)
  matrix products  42.5 us (4%)
  other arithmetic  25.1 us (2%)
    psum x1, blocking collectives, local(): raw_sum = lax.psum(bias_part, ('grp', 'seq'))  257 us
    all_to_all x1, waiting for transfers between devices, local(): lax.all_to_all(part_send, 'seq', split_axis=0, concat_axis=0, tiled=True)  171 us
    ppermute x3, waiting for transfers between devices, passed_along(): return lax.ppermute(block, axis, route)  171 us
    all_to_all x1, waiting for transfers between devices, local(): lax.all_to_all(q_send, 'seq', split_axis=0, concat_axis=0, tiled=True)  87 us
    all_to_all x1, waiting for transfers between devices, local(): lax.all_to_all(g_send, 'seq', split_axis=0, concat_axis=0, tiled=True)  69.2 us
    unnamed x26, local copies, waits for them, and re-layouts  44.6 us
    dot_general x14, matrix products, select_rows(): jnp.dot(picker.astype(lookup.dtype), lookup, preferred_element_type=jnp.f...  32.4 us
  transfers between devices with their start and end apart: 11, of which 9 were waited for; matrix products, arithmetic and copies ran while one was open for 10% of the time, Pallas kernels for 0%

commit v1 on v0

--- a/solution.py
+++ b/solution.py
@@ -199,7 +199,7 @@
     grad_before = passed_along(grad_win[tok_rows - STRETCH :], "seq", 1)
     attended = jnp.concatenate([att_before[1:], att_win[: tok_rows - STRETCH + 1]])
     d_query = jnp.concatenate([grad_before[1:], grad_win[: tok_rows - STRETCH + 1]])
-    raw_sum = lax.psum(bias_part, ("grp", "seq"))
+    raw_sum = lax.psum(lax.psum(bias_part, "grp"), "seq")
     squares = lax.psum(jnp.sum(raw_sum * raw_sum), "mp")
     d_bias = raw_sum * jnp.minimum(1.0, 1.0 / jnp.sqrt(squares + 1e-12))
     return (attended[None], d_query[None], d_kv[None], d_bias)

time: 1040 us -> 846 us (0.81)
  blocking collectives: 266 us -> 75 us
    psum x1 -> x2, blocking collectives: 257 us -> 65.9 us  [local(): raw_sum = lax.psum(lax.psum(bias_part, 'grp'), 'seq')]
  transfers between devices with their start and end apart: 11 -> 11, of which waited for: 9 -> 9; matrix products, arithmetic and copies ran while one was open for 10% -> 12% of each run, Pallas kernels for 0% -> 0%
where the time goes in v1:
time: 846 us; the launch traced here: 835 us
  waiting for transfers between devices  522 us (62%)
  local copies, waits for them, and re-layouts  90.5 us (11%)
  starting transfers between devices  77.4 us (9%)
  blocking collectives  75 us (9%)
  matrix products  42.5 us (5%)
  other arithmetic  25.1 us (3%)
    all_to_all x1, waiting for transfers between devices, local(): lax.all_to_all(part_send, 'seq', split_axis=0, concat_axis=0, tiled=True)  171 us
    ppermute x3, waiting for transfers between devices, passed_along(): return lax.ppermute(block, axis, route)  170 us
    all_to_all x1, waiting for transfers between devices, local(): lax.all_to_all(q_send, 'seq', split_axis=0, concat_axis=0, tiled=True)  87 us
    all_to_all x1, waiting for transfers between devices, local(): lax.all_to_all(g_send, 'seq', split_axis=0, concat_axis=0, tiled=True)  69.2 us
    psum x2, blocking collectives, local(): raw_sum = lax.psum(lax.psum(bias_part, 'grp'), 'seq')  65.9 us
    unnamed x26, local copies, waits for them, and re-layouts  44.6 us
    dot_general x14, matrix products, select_rows(): jnp.dot(picker.astype(lookup.dtype), lookup, preferred_element_type=jnp.f...  32.4 us
  transfers between devices with their start and end apart: 11, of which 9 were waited for; matrix products, arithmetic and copies ran while one was open for 12% of the time, Pallas kernels for 0%

profile of v1, /device:TPU:1, one launch (start us, length us, event | category | flops | bytes accessed | tf_op | source)
XLA Modules:
  0.0 834.7 jit_solution(17391214607842558193)
XLA Ops:
  4.3 16.7 %all-to-all-start = ((s32[32,1,1]{2,1,0:T(1,128)}), s32[32,1,1]{2,1,0:T(1,128)S(1)}, u32[]{:S(2)}, u32[]{:S(2)}) async-start(s32[32,1,1]{2,1,0:T(1,128)} %copy.156), calls=%async_computation | async-start | bytes 32768 | tf_op jit(solution)/shard_map/all_to_all | solution.py:92
  22.7 2.1 collective-permute-start
  24.9 7.8 all-to-all-done
  36.4 2.9 reduce.9
  39.3 4.5 reshape.685
  43.8 6.9 all-to-all-start.1
  51.2 2.1 fusion.1
  53.3 4.5 reduce.10
  57.8 4.5 reshape.687
  62.3 87.0 %all-to-all-done.1 = bf16[32,2,16384]{2,1,0:T(2,128)(2,1)S(1)} async-done(((bf16[32,2,16384]{2,1,0:T(2,128)(2,1)}), bf16[32,2,16384]{2,1,0:T(2,128)(2,1)S(1)}, u32[]{:S(2)}, u32[]{:S(2)}) %all-to-all-start.1) | async-done | bytes 2097184 | tf_op jit(solution)/shard_map/all_to_all | solution.py:105
  149.3 5.2 all-to-all-start.6
  154.5 6.2 copy.158
  161.5 2.7 fusion.78
  164.1 10.5 %reshape.686 = bf16[32,1,32768]{2,1,0:T(2,128)(2,1)} reshape(bf16[32,2,16384]{2,1,0:T(2,128)(2,1)} %copy-done) | data formatting | bytes 4194304
  174.6 4.5 convolution_convert_fusion.3
  179.9 1.9 fusion.79
  184.6 69.2 %all-to-all-done.6 = bf16[32,2,16384]{2,1,0:T(2,128)(2,1)} async-done(((bf16[32,2,16384]{2,1,0:T(2,128)(2,1)}), bf16[32,2,16384]{2,1,0:T(2,128)(2,1)}, u32[]{:S(2)}, u32[]{:S(2)}) %all-to-all-start.6) | async-done | bytes 2097184 | tf_op jit(solution)/shard_map/all_to_all | solution.py:106
  253.8 6.3 all-to-all-start.2
  260.7 2.9 copy.167
  263.6 2.7 reshape.655
  267.3 5.0 all-to-all-done.2
  272.3 7.3 all-to-all-start.4
  279.6 3.1 convolution_bitcast_fusion.1
  282.7 6.3 copy.168
  289.0 2.7 all-to-all-done.4
  291.7 9.9 %all-to-all-start.3 = ((f32[32,1,32768]{2,1,0:T(1,128)}), f32[32,1,32768]{2,1,0:T(1,128)}, u32[]{:S(2)}, u32[]{:S(2)}) async-start(f32[32,1,32768]{2,1,0:T(1,128)} %copy.168), calls=%async_computation.3 | async-start | bytes 8388608 | tf_op jit(solution)/shard_map/all_to_all | solution.py:134
  301.7 10.5 %reshape.688 = bf16[32,1,32768]{2,1,0:T(2,128)(2,1)} reshape(bf16[32,2,16384]{2,1,0:T(2,128)(2,1)} %all-to-all-done.6) | data formatting | bytes 4194304
  313.4 171.4 %all-to-all-done.3 = f32[32,1,32768]{2,1,0:T(1,128)} async-done(((f32[32,1,32768]{2,1,0:T(1,128)}), f32[32,1,32768]{2,1,0:T(1,128)}, u32[]{:S(2)}, u32[]{:S(2)}) %all-to-all-start.3) | async-done | bytes 4194336 | tf_op jit(solution)/shard_map/all_to_all | solution.py:134
  484.7 6.6 copy.249
  491.3 6.0 dot_general.86
  497.4 6.8 fusion.20
  506.6 10.9 %all-to-all-start.5 = ((f32[32,1,512]{2,1,0:T(1,128)}), f32[32,1,512]{2,1,0:T(1,128)S(1)}, u32[]{:S(2)}, u32[]{:S(2)}) async-start(f32[32,1,512]{2,1,0:T(1,128)} %copy.177), calls=%async_computation.5 | async-start | bytes 131072 | tf_op jit(solution)/shard_map/all_to_all | solution.py:159
  517.5 4.5 convolution_convert_fusion.2
  522.0 8.5 %all-to-all-done.5 = f32[32,1,512]{2,1,0:T(1,128)S(1)} async-done(((f32[32,1,512]{2,1,0:T(1,128)}), f32[32,1,512]{2,1,0:T(1,128)S(1)}, u32[]{:S(2)}, u32[]{:S(2)}) %all-to-all-start.5) | async-done | bytes 65568 | tf_op jit(solution)/shard_map/all_to_all | solution.py:159
  532.7 2.0 fusion.12
  537.0 3.1 convolution_bitcast_fusion
  540.1 6.3 copy.187
  546.4 6.1 all-to-all-start.7
  552.9 3.7 collective-permute-start.1
  556.7 169.2 %collective-permute-done.1 = bf16[64,512]{1,0:T(8,128)(2,1)S(1)} collective-permute-done((bf16[64,512]{1,0:T(8,128)(2,1)S(1)}, bf16[64,512]{1,0:T(8,128)(2,1)S(1)}, u32[]{:S(2)}, u32[]{:S(2)}) %collective-permute-start.1) | collective-permute-done | bytes 65568 | tf_op jit(solution)/shard_map/ppermute | solution.py:13
  726.5 9.1 %psum.21 = f32[4,191]{1,0:T(4,128)S(1)} all-reduce(f32[4,191]{1,0:T(4,128)S(1)} %reduce_sum.88), channel_id=1, replica_groups=mesh['grp'=4,'seq'=32,'mp'=4] {'grp'}, use_global_device_ids=true, to_apply=%region_10.11 | all-reduce | flops 764 | bytes 6112 | tf_op jit(solution)/shard_map/psum | solution.py:202
  735.6 56.8 %psum.22 = f32[4,191]{1,0:T(4,128)S(1)} all-reduce(f32[4,191]{1,0:T(4,128)S(1)} %psum.21), channel_id=1, replica_groups=mesh['grp'=4,'seq'=32,'mp'=4] {'seq'}, use_global_device_ids=true, to_apply=%region_11.12 | all-reduce | flops 764 | bytes 6112 | tf_op jit(solution)/shard_map/psum | solution.py:202
  793.7 9.1 %psum.23 = f32[]{:T(128)} all-reduce(f32[]{:T(128)} %multiply_reduce_fusion.1), channel_id=1, replica_groups=mesh['grp'=4,'seq'=32,'mp'=4] {'mp'}, use_global_device_ids=true, to_apply=%region_13.14 | all-reduce | flops 1 | bytes 8 | tf_op jit(solution)/shard_map/psum | solution.py:203
  804.6 4.6 copy.191
  811.0 3.8 copy.190
  815.5 6.7 pad_maximum_fusion
  822.2 6.0 fusion.2
  829.6 2.2 collective-permute-start.2
  (116 shorter events, 33.3 us)
Async XLA Ops:
  4.3 28.5 %all-to-all-start = ((s32[32,1,1]{2,1,0:T(1,128)}), s32[32,1,1]{2,1,0:T(1,128)S(1)}, u32[]{:S(2)}, u32[]{:S(2)}) async-start(s32[32,1,1]{2,1,0:T(1,128)} %copy.156), calls=%async_computation | async-start | bytes 32768 | tf_op jit(solution)/shard_map/all_to_all | solution.py:92
  22.7 11.4 %collective-permute-start = (bf16[2,64,512]{2,1,0:T(8,128)(2,1)S(1)}, bf16[2,64,512]{2,1,0:T(8,128)(2,1)S(1)}, u32[]{:S(2)}, u32[]{:S(2)}) collective-permute-start(bf16[2,64,512]{2,1,0:T(8,128)(2,1)S(1)} %pad_maximum_fusion.3), channel_id=1, source_target_pairs={{4,0},{8,4},{12,8},{16,12},{20,16},{24,20},{28,24},{32,28},{36,32}... | collective-permute-start | bytes 393224 | tf_op jit(solution)/shard_map/ppermute | solution.py:13
  39.3 11.7 %copy-start.5 = (bf16[1,128,512]{2,1,0:T(8,128)(2,1)S(1)}, bf16[1,128,512]{2,1,0:T(8,128)(2,1)}, u32[]{:S(2)}) copy-start(bf16[1,128,512]{2,1,0:T(8,128)(2,1)} %param.6) | copy-start | bytes 393220
  43.8 105.5 %all-to-all-start.1 = ((bf16[32,2,16384]{2,1,0:T(2,128)(2,1)}), bf16[32,2,16384]{2,1,0:T(2,128)(2,1)S(1)}, u32[]{:S(2)}, u32[]{:S(2)}) async-start(bf16[32,2,16384]{2,1,0:T(2,128)(2,1)} %reshape.685), calls=%async_computation.1 | async-start | bytes 4194304 | tf_op jit(solution)/shard_map/all_to_all | solution.py:105
  62.3 98.4 %copy-start.7 = (f32[4,191]{1,0:T(4,128)S(1)}, f32[4,191]{1,0:T(4,128)}, u32[]{:S(2)}) copy-start(f32[4,191]{1,0:T(4,128)} %param.9) | copy-start | bytes 9172
  149.3 11.4 %copy-start = (bf16[32,2,16384]{2,1,0:T(2,128)(2,1)}, bf16[32,2,16384]{2,1,0:T(2,128)(2,1)S(1)}, u32[]{:S(2)}) copy-start(bf16[32,2,16384]{2,1,0:T(2,128)(2,1)S(1)} %all-to-all-done.1) | copy-start | bytes 6291460
  149.3 104.5 %all-to-all-start.6 = ((bf16[32,2,16384]{2,1,0:T(2,128)(2,1)}), bf16[32,2,16384]{2,1,0:T(2,128)(2,1)}, u32[]{:S(2)}, u32[]{:S(2)}) async-start(bf16[32,2,16384]{2,1,0:T(2,128)(2,1)} %reshape.687), calls=%async_computation.6 | async-start | bytes 4194304 | tf_op jit(solution)/shard_map/all_to_all | solution.py:106
  179.1 0.8 copy-start.4
  253.8 18.5 %all-to-all-start.2 = ((f32[32,1,256]{2,1,0:T(1,128)}), f32[32,1,256]{2,1,0:T(1,128)S(1)}, u32[]{:S(2)}, u32[]{:S(2)}) async-start(f32[32,1,256]{2,1,0:T(1,128)} %copy.162), calls=%async_computation.2 | async-start | bytes 65536 | tf_op jit(solution)/shard_map/all_to_all | solution.py:135
  272.3 19.4 %all-to-all-start.4 = ((f32[32,1,256]{2,1,0:T(1,128)}), f32[32,1,256]{2,1,0:T(1,128)S(1)}, u32[]{:S(2)}, u32[]{:S(2)}) async-start(f32[32,1,256]{2,1,0:T(1,128)} %copy.171), calls=%async_computation.4 | async-start | bytes 65536 | tf_op jit(solution)/shard_map/all_to_all | solution.py:136
  291.7 193.0 %all-to-all-start.3 = ((f32[32,1,32768]{2,1,0:T(1,128)}), f32[32,1,32768]{2,1,0:T(1,128)}, u32[]{:S(2)}, u32[]{:S(2)}) async-start(f32[32,1,32768]{2,1,0:T(1,128)} %copy.168), calls=%async_computation.3 | async-start | bytes 8388608 | tf_op jit(solution)/shard_map/all_to_all | solution.py:134
  506.6 23.9 %all-to-all-start.5 = ((f32[32,1,512]{2,1,0:T(1,128)}), f32[32,1,512]{2,1,0:T(1,128)S(1)}, u32[]{:S(2)}, u32[]{:S(2)}) async-start(f32[32,1,512]{2,1,0:T(1,128)} %copy.177), calls=%async_computation.5 | async-start | bytes 131072 | tf_op jit(solution)/shard_map/all_to_all | solution.py:159
  522.0 13.5 %copy-start.1 = (bf16[8,32768]{1,0:T(8,128)(2,1)}, bf16[8,32768]{1,0:T(8,128)(2,1)S(1)}, u32[]{:S(2)}) copy-start(bf16[8,32768]{1,0:T(8,128)(2,1)S(1)} %convolution_convert_fusion.2) | copy-start | bytes 1572868
  531.9 0.8 copy-start.3
  546.4 6.4 copy-start.6
  546.4 256.4 %copy-start.2 = (bf16[8,32768]{1,0:T(8,128)(2,1)S(1)}, bf16[8,32768]{1,0:T(8,128)(2,1)}, u32[]{:S(2)}) copy-start(bf16[8,32768]{1,0:T(8,128)(2,1)} %copy-done.1) | copy-start | bytes 1572868
  546.4 275.8 %all-to-all-start.7 = ((f32[32,1,32768]{2,1,0:T(1,128)}), f32[32,1,32768]{2,1,0:T(1,128)}, u32[]{:S(2)}, u32[]{:S(2)}) async-start(f32[32,1,32768]{2,1,0:T(1,128)} %copy.187), calls=%async_computation.7 | async-start | bytes 8388608 | tf_op jit(solution)/shard_map/all_to_all | solution.py:193
  552.9 173.0 %collective-permute-start.1 = (bf16[64,512]{1,0:T(8,128)(2,1)S(1)}, bf16[64,512]{1,0:T(8,128)(2,1)S(1)}, u32[]{:S(2)}, u32[]{:S(2)}) collective-permute-start(bf16[64,512]{1,0:T(8,128)(2,1)S(1)} %bitcast.224), channel_id=1, source_target_pairs={{0,4},{4,8},{8,12},{12,16},{16,20},{20,24},{24,28},{28,32},{32,36}... | collective-permute-start | bytes 196616 | tf_op jit(solution)/shard_map/ppermute | solution.py:13
  829.6 4.2 collective-permute-start.2
